TPU v7x, 256 devices: a whole 4x4x8 slice. The times are simulated.
256 devices in a mesh: bus: 16 (over y, z_hi), line: 16 (over z_lo, x, core).
Axes of the slice: x: 4, y: 4, z: 8 (z_hi: 4, z_lo: 2; z = z_hi * 2 + z_lo), core: 2. Of those that a mesh axis runs over, the one named last changes fastest.
Arguments:
- generation: bfloat16 [1024, 16384], P(None, 'bus'), may hold values from -6 to 6
- profiles: float32 [24, 16384], P(None, 'bus'), may hold values from -5 to 5
- scen_profile: int32 [1024], replicated, may hold values from 0 to 23
- ptdf: bfloat16 [16384, 16384], P('line', 'bus'), may hold values from -0.046875 to 0.046875
- lodf: float32 [6144, 512], P('line'), may hold values from -1 to 1
- limits: float32 [6144], P('line'), may hold values from 0.5 to 2
- monitored: int32 [6144], P('line'), may hold values from 0 to 16383, as said below
- outages: int32 [512], replicated, may hold values from 0 to 16383, as said below
- cost_quad: float32 [16384], P('bus'), may hold values from 0.5 to 2
Outputs:
- gradient: bfloat16 [1024, 16384], P('line', 'bus')
- outage_flow: float32 [1024, 512], P('bus')
- outage_sens: float32 [1024, 512], P('bus')
Inputs may be any that keep to these rules, and one draw needn't show every extreme that they name: `monitored`: the entries with positions k * 384 to (k + 1) * 384 - 1 are distinct line ids of the k-th block of 1024 lines (ids k * 1024 to (k + 1) * 1024 - 1). `outages`: distinct line ids; how many fall in each block of 1024 lines varies from block to block.
All inputs are finite; a program needn't handle non-finite values.
Results may differ from a plain program's by a relative error of at most 0.0029.
Values may be sent and summed in bfloat16 or wider, within the bound.
No kernel may reach another device: no remote copies, remote signals or barrier semaphores. Data moves between devices by JAX's collectives and lax.ppermute only.
A program may use at most 64 MiB of HBM per device.

v0:
```python
import math
import jax
import jax.numpy as jnp
from jax import lax
from jax.sharding import PartitionSpec as P

sharpness = 4.0


def contingency(pieces, lodf, limits, outage_total):
    base_block, outage_block = pieces
    post_flow = base_block[:, :, None] + lodf[None, :, :] * outage_block[:, None, :]
    bounds = limits[None, :, None]
    raw_slope = jax.nn.sigmoid(sharpness * (post_flow - bounds)) - jax.nn.sigmoid(
        sharpness * (-post_flow - bounds)
    )
    direct = jnp.sum(raw_slope, axis=2) / outage_total
    sens_part = jnp.einsum("smk,mk->sk", raw_slope, lodf, precision=lax.Precision.HIGHEST)
    return (direct, sens_part)


def on_device(
    generation, profiles, scen_profile, ptdf, lodf, limits, monitored, outages, cost_quad
):
    line_count = lax.axis_size("line")
    profile_count = profiles.shape[0]
    profile_pick = (
        scen_profile[:, None] == jnp.arange(profile_count, dtype=jnp.int32)[None, :]
    ).astype(jnp.float32)
    loads = jnp.dot(profile_pick, profiles, precision=lax.Precision.HIGHEST)
    injection = (generation.astype(jnp.float32) - loads).astype(jnp.bfloat16)
    scen_rows = injection.shape[0] // lax.axis_size("bus")
    line_rows = ptdf.shape[0]
    first_line = lax.axis_index("line") * line_rows
    local_monitored = monitored - first_line
    monitor_count = monitored.shape[0]
    outage_total = outages.shape[0]
    monitored_total = monitor_count * line_count
    rel_outages = outages - first_line
    in_block = (rel_outages >= 0) & (rel_outages < line_rows)
    outage_rows = jnp.where(
        in_block[:, None],
        jnp.take(ptdf, jnp.clip(rel_outages, 0, line_rows - 1), axis=0),
        jnp.zeros((), ptdf.dtype),
    )
    my_outage_rows = lax.psum_scatter(outage_rows, "line", scatter_dimension=0, tiled=True)
    monitored_rows = jnp.take(ptdf, local_monitored, axis=0)
    rows = jnp.concatenate([monitored_rows, my_outage_rows], axis=0)
    flow_part = lax.dot_general(
        injection, rows, (((1,), (1,)), ((), ())), preferred_element_type=jnp.float32
    )
    flow_field = lax.psum_scatter(flow_part, "bus", scatter_dimension=0, tiled=True)
    base = flow_field[:, :monitor_count]
    outflow = lax.all_gather(flow_field[:, monitor_count:], "line", axis=1, tiled=True)
    block_size = math.gcd(scen_rows, 4)
    base_blocks = base.reshape(scen_rows // block_size, block_size, monitor_count)
    outage_blocks = outflow.reshape(scen_rows // block_size, block_size, outage_total)
    direct, sens_part = lax.map(
        lambda pieces: contingency(pieces, lodf, limits, outage_total), (base_blocks, outage_blocks)
    )
    direct = direct.reshape(scen_rows, monitor_count)
    sens_part = sens_part.reshape(scen_rows, outage_total)
    matches = (outages[:, None] == monitored[None, :]).astype(jnp.float32)
    flag_part = jnp.sum(matches, axis=1)
    extended = jnp.concatenate(
        [sens_part, flag_part[None, :], jnp.zeros((7, outage_total), jnp.float32)], axis=0
    )
    mine = lax.psum_scatter(extended, "line", scatter_dimension=1, tiled=True)
    sens_mine = mine[:scen_rows]
    flag_mine = mine[scen_rows]
    sens_total = lax.all_gather(sens_mine, "line", axis=1, tiled=True)
    backward = sens_total / outage_total
    outage_sens = sens_total / math.sqrt(monitored_total)
    adjoint_monitored = (
        direct + jnp.dot(backward, matches, precision=lax.Precision.HIGHEST)
    ).astype(jnp.bfloat16)
    adjoint_outage = jnp.where(flag_mine[None, :] > 0.5, 0.0, sens_mine / outage_total).astype(
        jnp.bfloat16
    )
    piece = jnp.concatenate([adjoint_monitored, adjoint_outage], axis=1)
    all_piece = lax.all_gather(piece, "bus", axis=0, tiled=True)
    grad_rows = all_piece.shape[0] // line_count
    pushed = lax.psum_scatter(
        jnp.dot(all_piece, rows, preferred_element_type=jnp.float32),
        "line",
        scatter_dimension=0,
        tiled=True,
    )
    own_generation = lax.dynamic_slice_in_dim(
        generation, lax.axis_index("line") * grad_rows, grad_rows, 0
    ).astype(jnp.float32)
    gradient = (cost_quad[None, :] * own_generation + pushed).astype(jnp.bfloat16)
    return (gradient, outflow, outage_sens)


def solution(mesh):
    placed = (
        P(None, "bus"),
        P(None, "bus"),
        P(),
        P("line", "bus"),
        P("line", None),
        P("line"),
        P("line"),
        P(),
        P("bus"),
    )
    return jax.shard_map(
        on_device,
        mesh=mesh,
        in_specs=placed,
        out_specs=(P("line", "bus"), P("bus", None), P("bus", None)),
        check_vma=False,
    )
```

profile of v0, /device:TPU:16, one launch (start us, length us, event | category | flops | bytes accessed | tf_op | source)
XLA Modules:
  0.0 532.0 jit_solution(728160581816020870)
XLA Ops:
  8.8 2.0 gather_fusion.1
  10.8 1.2 select_select_fusion
  12.2 2.1 gather_fusion
  14.3 1.0 broadcast_select_fusion
  15.3 4.9 subtract_convert_fusion
  20.2 59.7 %reduce-scatter.7.cloned.1.call-done = bf16[32,1024]{1,0:T(8,128)(2,1)} async-done(((bf16[512,1024]{1,0:T(8,128)(2,1)}), bf16[32,1024]{1,0:T(8,128)(2,1)}) %reduce-scatter.7.cloned.1.call-update) | async-done | bytes 65552 | tf_op jit(solution)/shard_map/reduce_scatter | solution.py:46
  80.0 4.2 fusion.5
  84.6 86.4 %reduce-scatter.9.cloned.1.call-done = f32[64,416]{1,0:T(8,128)} async-done(((f32[1024,416]{1,0:T(8,128)}), f32[64,416]{1,0:T(8,128)}) %reduce-scatter.9.cloned.1.call-update) | async-done | bytes 106512 | tf_op jit(solution)/shard_map/reduce_scatter | solution.py:52
  172.7 19.4 %all_gather.9 = f32[64,512]{0,1:T(8,128)S(1)} all-gather(f32[64,32]{0,1:T(8,128)S(1)} %copy.22), channel_id=1, replica_groups=mesh['bus'=16,'line'=16] {'line'}, dimensions={1}, use_global_device_ids=true | all-gather | bytes 139264 | tf_op jit(solution)/shard_map/all_gather | solution.py:54
  192.9 128.0 %while.12 = (s32[]{:T(128)}, f32[16,4,384]{2,1,0:T(4,128)}, f32[16,4,512]{2,1,0:T(4,128)}, f32[16,4,384]{2,1,0:T(4,128)S(1)}, f32[384,512]{1,0:T(8,128)}, /*inde...) while((s32[]{:T(128)}, f32[16,4,384]{2,1,0:T(4,128)}, f32[16,4,512]{2,1,0:T(4,128)}, ...), condition=%wide.region_4.5_spmd, body=%wide.region_2.4_spmd.sunk | while | flops 24377344 | bytes 2462829 | solution.py:58
  192.9 3.3 fusion.18
  196.2 3.5 multiply_reduce_fusion.2
  200.9 3.3 fusion.18
  204.2 3.5 multiply_reduce_fusion.2
  208.9 3.3 fusion.18
  212.2 3.5 multiply_reduce_fusion.2
  216.9 3.3 fusion.18
  220.2 3.5 multiply_reduce_fusion.2
  224.9 3.3 fusion.18
  228.2 3.5 multiply_reduce_fusion.2
  232.9 3.3 fusion.18
  236.2 3.5 multiply_reduce_fusion.2
  240.9 3.3 fusion.18
  244.2 3.5 multiply_reduce_fusion.2
  248.9 3.3 fusion.18
  252.2 3.5 multiply_reduce_fusion.2
  256.9 3.3 fusion.18
  260.2 3.5 multiply_reduce_fusion.2
  264.9 3.3 fusion.18
  268.2 3.5 multiply_reduce_fusion.2
  272.9 3.3 fusion.18
  276.2 3.5 multiply_reduce_fusion.2
  280.9 3.3 fusion.18
  284.2 3.5 multiply_reduce_fusion.2
  288.9 3.3 fusion.18
  292.2 3.5 multiply_reduce_fusion.2
  296.9 3.3 fusion.18
  300.2 3.5 multiply_reduce_fusion.2
  304.9 3.3 fusion.18
  308.2 3.5 multiply_reduce_fusion.2
  312.9 3.3 fusion.18
  316.2 3.5 multiply_reduce_fusion.2
  323.8 59.1 %reduce-scatter.13.cloned.1.call-done = f32[32,72]{1,0:T(8,128)} async-done(((f32[512,72]{1,0:T(8,128)}), f32[32,72]{1,0:T(8,128)}) %reduce-scatter.13.cloned.1.call-update) | async-done | bytes 9232
  384.5 16.9 %all_gather.10 = f32[64,512]{0,1:T(8,128)S(1)} all-gather(f32[64,32]{0,1:T(8,128)} %bitcast.36), channel_id=1, replica_groups=mesh['bus'=16,'line'=16] {'line'}, dimensions={1}, use_global_device_ids=true | all-gather | bytes 139264 | tf_op jit(solution)/shard_map/all_gather | solution.py:71
  402.1 44.6 %all_gather.11 = bf16[1024,416]{1,0:T(8,128)(2,1)S(1)} all-gather(bf16[64,416]{1,0:T(8,128)(2,1)S(1)} %pad_maximum_fusion.3), channel_id=1, replica_groups=mesh['bus'=16,'line'=16] {'bus'}, dimensions={0}, use_global_device_ids=true | all-gather | bytes 905216 | tf_op jit(solution)/shard_map/all_gather | solution.py:81
  446.7 3.2 fusion.4
  450.7 73.1 %reduce-scatter.11.cloned.1.call-done = f32[64,1024]{1,0:T(8,128)} async-done(((f32[1024,1024]{1,0:T(8,128)}), f32[64,1024]{1,0:T(8,128)}) %reduce-scatter.11.cloned.1.call-update) | async-done | bytes 262160 | tf_op jit(solution)/shard_map/reduce_scatter | solution.py:83
  523.8 1.7 add_convert_fusion
  (119 shorter events, 29.7 us)
Async XLA Ops:
  7.2 1.6 copy-start
  7.2 72.8 %reduce-scatter.7.cloned.1.call-start = ((), (), s32[]{:S(2)}) async-start(), calls=%async_computation.4 | async-start | bytes 1114112 | tf_op jit(solution)/shard_map/reduce_scatter | solution.py:46
  10.8 1.3 copy-start.4
  12.1 158.9 %reduce-scatter.9.cloned.1.call-start = ((), (), s32[]{:S(2)}) async-start(), calls=%async_computation.5 | async-start | bytes 2228224 | tf_op jit(solution)/shard_map/reduce_scatter | solution.py:52
  12.2 3.1 copy-start.3
  12.2 3.1 copy-start.6
  15.3 64.7 %copy-start.1 = (bf16[384,1024]{1,0:T(8,128)(2,1)S(1)}, bf16[384,1024]{1,0:T(8,128)(2,1)}, u32[]{:S(2)}) copy-start(bf16[384,1024]{1,0:T(8,128)(2,1)} %broadcast_select_fusion) | copy-start | bytes 2359300
  20.2 64.1 %copy-start.5 = (s32[512]{0:T(512)S(1)}, s32[512]{0:T(512)}, u32[]{:S(2)}) copy-start(s32[512]{0:T(512)} %param.18) | copy-start | bytes 6148
  84.2 108.1 %copy-start.9 = (f32[384]{0:T(512)S(1)}, f32[384]{0:T(512)}, u32[]{:S(2)}) copy-start(f32[384]{0:T(512)} %param.16) | copy-start | bytes 4612
  84.2 298.7 %reduce-scatter.13.cloned.1.call-start = ((), (), s32[]{:S(2)}) async-start(), calls=%async_computation.7 | async-start | bytes 278528
  192.2 0.7 copy-start.2
  320.9 125.8 %copy-start.8 = (bf16[32,1024]{1,0:T(8,128)(2,1)S(1)}, bf16[32,1024]{1,0:T(8,128)(2,1)}, u32[]{:S(2)}) copy-start(bf16[32,1024]{1,0:T(8,128)(2,1)} %reduce-scatter.7.cloned.1.call-done) | copy-start | bytes 196612
  322.8 201.0 %reduce-scatter.11.cloned.1.call-start = ((), (), s32[]{:S(2)}) async-start(), calls=%async_computation.6 | async-start | bytes 4456448 | tf_op jit(solution)/shard_map/reduce_scatter | solution.py:83
  449.9 73.9 %copy-start.7 = (f32[1024]{0:T(1024)S(1)}, f32[1024]{0:T(1024)}, u32[]{:S(2)}) copy-start(f32[1024]{0:T(1024)} %param.19) | copy-start | bytes 12292
Sparse Core Ops, SparseCore 0:
  12.2 67.7 reduce-scatter.6
  84.3 86.6 reduce-scatter.8
  322.9 59.9 reduce-scatter.12
  450.0 73.7 reduce-scatter.10
where the time goes:
time: 534 us; the launch traced here: 532 us
  waiting for transfers between devices  278 us (52%)
  other arithmetic  124 us (23%)
  blocking collectives  80.9 us (15%)
  local copies, waits for them, and re-layouts  21.5 us (4%)
  between operations  13.9 us (3%)
  matrix products  12.8 us (2%)
    reduce_scatter x1, waiting for transfers between devices, on_device(): lax.psum_scatter(flow_part, 'bus', scatter_dimension=0, tiled=True)  86.4 us
    reduce_scatter x1, waiting for transfers between devices, on_device(): lax.psum_scatter(jnp.dot(all_piece, rows, preferred_element_type=jnp.floa...  73.1 us
    reduce_scatter x1, waiting for transfers between devices, on_device(): lax.psum_scatter(outage_rows, 'line', scatter_dimension=0, tiled=True)  59.7 us
    unnamed x5, waiting for transfers between devices  59.2 us
    dot_general x16, other arithmetic, contingency(): jnp.einsum('smk,mk->sk', raw_slope, lodf, precision=lax.Precision.HIGHEST)  55.3 us
    reduce_sum x16, other arithmetic, contingency(): direct = jnp.sum(raw_slope, axis=2) / outage_total  53.3 us
    all_gather x1, blocking collectives, on_device(): all_piece = lax.all_gather(piece, 'bus', axis=0, tiled=True)  44.6 us
    all_gather x1, blocking collectives, on_device(): lax.all_gather(flow_field[:, monitor_count:], 'line', axis=1, tiled=True)  19.4 us
  transfers between devices with their start and end apart: 4, of which 4 were waited for; matrix products, arithmetic and copies ran while one was open for 2% of the time, Pallas kernels for 0%

commit v1 on v0

--- a/solution.py
+++ b/solution.py
@@ -51,7 +51,12 @@
     )
     flow_field = lax.psum_scatter(flow_part, "bus", scatter_dimension=0, tiled=True)
     base = flow_field[:, :monitor_count]
-    outflow = lax.all_gather(flow_field[:, monitor_count:], "line", axis=1, tiled=True)
+    outflow = jnp.concatenate(
+        lax.all_to_all(
+            jnp.stack([flow_field[:, monitor_count:]] * lax.axis_size("line")), "line", 0, 0
+        ),
+        axis=1,
+    )
     block_size = math.gcd(scen_rows, 4)
     base_blocks = base.reshape(scen_rows // block_size, block_size, monitor_count)
     outage_blocks = outflow.reshape(scen_rows // block_size, block_size, outage_total)

time: 534 us -> 516 us (0.966)
  blocking collectives: 80.9 us -> 64.8 us
  local copies, waits for them, and re-layouts: 21.5 us -> 13.1 us
    all_gather x1 -> x0, blocking collectives: 19.4 us -> none  [on_device(): lax.all_gather(flow_field[:, monitor_count:], 'line', axis=1, tiled=True)]
    dynamic_update_slice x16, local copies, waits for them, and re-layouts: 9.57 us -> 0.12 us  [on_device(): lax.map(lambda pieces: contingency(pieces, lodf, limits, outage_total), (...]
    reduce_scatter x1, waiting for transfers between devices: 73.1 us -> 66.7 us  [on_device(): lax.psum_scatter(jnp.dot(all_piece, rows, preferred_element_type=jnp.floa...]
    all_to_all x0 -> x1, waiting for transfers between devices: none -> 5.34 us  [on_device(): lax.all_to_all(jnp.stack([flow_field[:, monitor_count:]] * lax.axis_size(...]
  transfers between devices with their start and end apart: 4 -> 5, of which waited for: 4 -> 5; matrix products, arithmetic and copies ran while one was open for 2% -> 2% of each run, Pallas kernels for 0% -> 0%
where the time goes in v1:
time: 516 us; the launch traced here: 514 us
  waiting for transfers between devices  278 us (54%)
  other arithmetic  126 us (24%)
  blocking collectives  64.8 us (13%)
  between operations  14 us (3%)
  matrix products  13.6 us (3%)
  local copies, waits for them, and re-layouts  13.1 us (3%)
    reduce_scatter x1, waiting for transfers between devices, on_device(): lax.psum_scatter(flow_part, 'bus', scatter_dimension=0, tiled=True)  86.7 us
    reduce_scatter x1, waiting for transfers between devices, on_device(): lax.psum_scatter(jnp.dot(all_piece, rows, preferred_element_type=jnp.floa...  66.7 us
    reduce_scatter x1, waiting for transfers between devices, on_device(): lax.psum_scatter(outage_rows, 'line', scatter_dimension=0, tiled=True)  59.7 us
    unnamed x5, waiting for transfers between devices  59.6 us
    dot_general x16, other arithmetic, contingency(): jnp.einsum('smk,mk->sk', raw_slope, lodf, precision=lax.Precision.HIGHEST)  56 us
    reduce_sum x16, other arithmetic, contingency(): direct = jnp.sum(raw_slope, axis=2) / outage_total  53.4 us
    all_gather x1, blocking collectives, on_device(): all_piece = lax.all_gather(piece, 'bus', axis=0, tiled=True)  47.8 us
    all_gather x1, blocking collectives, on_device(): sens_total = lax.all_gather(sens_mine, 'line', axis=1, tiled=True)  16.9 us
  transfers between devices with their start and end apart: 5, of which 5 were waited for; matrix products, arithmetic and copies ran while one was open for 2% of the time, Pallas kernels for 0%

profile of v1, /device:TPU:16, one launch (start us, length us, event | category | flops | bytes accessed | tf_op | source)
XLA Modules:
  0.0 514.4 jit_solution(11879025675101448193)
XLA Ops:
  8.8 2.0 gather_fusion.1
  10.8 1.2 select_select_fusion
  12.2 2.1 gather_fusion
  15.3 4.9 subtract_convert_fusion
  20.3 59.7 %reduce-scatter.7.cloned.1.call-done = bf16[32,1024]{1,0:T(8,128)(2,1)} async-done(((bf16[512,1024]{1,0:T(8,128)(2,1)}), bf16[32,1024]{1,0:T(8,128)(2,1)}) %reduce-scatter.7.cloned.1.call-update) | async-done | bytes 65552 | tf_op jit(solution)/shard_map/reduce_scatter | solution.py:46
  80.0 4.2 fusion.5
  84.2 86.7 %reduce-scatter.9.cloned.1.call-done = f32[64,416]{1,0:T(8,128)} async-done(((f32[1024,416]{1,0:T(8,128)}), f32[64,416]{1,0:T(8,128)}) %reduce-scatter.9.cloned.1.call-update) | async-done | bytes 106512 | tf_op jit(solution)/shard_map/reduce_scatter | solution.py:52
  172.6 4.5 all-to-all-start
  178.4 5.3 %all-to-all-done = f32[16,1,2048]{2,1,0:T(1,128)S(1)} async-done(((f32[16,1,2048]{2,1,0:T(1,128)}), f32[16,1,2048]{2,1,0:T(1,128)S(1)}, u32[]{:S(2)}, u32[]{:S(2)}) %all-to-all-start) | async-done | bytes 131104 | tf_op jit(solution)/shard_map/all_to_all | solution.py:55
  185.9 119.4 %while.12 = (s32[]{:T(128)}, f32[16,4,384]{2,1,0:T(4,128)}, f32[16,4,512]{2,1,0:T(4,128)S(1)}, f32[16,4,384]{2,1,0:T(4,128)S(1)}, f32[384,512]{1,0:T(8,128)}, /*...) while((s32[]{:T(128)}, f32[16,4,384]{2,1,0:T(4,128)}, f32[16,4,512]{2,1,0:T(4,128)S(1)}, ...), condition=%wide.region_4.5_spmd, body=%wide.region_2.4_spmd.sunk | while | flops 24377344 | bytes 2462829 | solution.py:63
  186.0 3.3 fusion.18
  189.3 3.5 multiply_reduce_fusion.2
  193.4 3.3 fusion.18
  196.8 3.5 multiply_reduce_fusion.2
  200.9 3.3 fusion.18
  204.2 3.5 multiply_reduce_fusion.2
  208.4 3.3 fusion.18
  211.7 3.5 multiply_reduce_fusion.2
  215.8 3.3 fusion.18
  219.2 3.5 multiply_reduce_fusion.2
  223.3 3.3 fusion.18
  226.6 3.5 multiply_reduce_fusion.2
  230.7 3.3 fusion.18
  234.1 3.5 multiply_reduce_fusion.2
  238.2 3.3 fusion.18
  241.5 3.5 multiply_reduce_fusion.2
  245.6 3.3 fusion.18
  249.0 3.5 multiply_reduce_fusion.2
  253.1 3.3 fusion.18
  256.4 3.5 multiply_reduce_fusion.2
  260.6 3.3 fusion.18
  263.9 3.5 multiply_reduce_fusion.2
  268.0 3.3 fusion.18
  271.4 3.5 multiply_reduce_fusion.2
  275.5 3.3 fusion.18
  278.8 3.5 multiply_reduce_fusion.2
  282.9 3.3 fusion.18
  286.3 3.5 multiply_reduce_fusion.2
  290.4 3.3 fusion.18
  293.7 3.5 multiply_reduce_fusion.2
  297.8 3.3 fusion.18
  301.2 3.5 multiply_reduce_fusion.2
  307.3 59.5 %reduce-scatter.13.cloned.1.call-done = f32[32,72]{1,0:T(8,128)} async-done(((f32[512,72]{1,0:T(8,128)}), f32[32,72]{1,0:T(8,128)}) %reduce-scatter.13.cloned.1.call-update) | async-done | bytes 9232
  368.4 16.9 %all_gather.6 = f32[64,512]{0,1:T(8,128)S(1)} all-gather(f32[64,32]{0,1:T(8,128)} %bitcast.45), channel_id=1, replica_groups=mesh['bus'=16,'line'=16] {'line'}, dimensions={1}, use_global_device_ids=true | all-gather | bytes 139264 | tf_op jit(solution)/shard_map/all_gather | solution.py:76
  386.0 47.8 %all_gather.7 = bf16[1024,416]{1,0:T(8,128)(2,1)S(1)} all-gather(bf16[64,416]{1,0:T(8,128)(2,1)S(1)} %pad_maximum_fusion.3), channel_id=1, replica_groups=mesh['bus'=16,'line'=16] {'bus'}, dimensions={0}, use_global_device_ids=true | all-gather | bytes 905216 | tf_op jit(solution)/shard_map/all_gather | solution.py:86
  433.8 4.0 fusion.4
  439.4 66.7 %reduce-scatter.11.cloned.1.call-done = f32[64,1024]{1,0:T(8,128)} async-done(((f32[1024,1024]{1,0:T(8,128)}), f32[64,1024]{1,0:T(8,128)}) %reduce-scatter.11.cloned.1.call-update) | async-done | bytes 262160 | tf_op jit(solution)/shard_map/reduce_scatter | solution.py:88
  506.2 1.7 add_convert_fusion
  (125 shorter events, 23.4 us)
Async XLA Ops:
  7.2 1.6 copy-start
  7.2 72.8 %reduce-scatter.7.cloned.1.call-start = ((), (), s32[]{:S(2)}) async-start(), calls=%async_computation.5 | async-start | bytes 1114112 | tf_op jit(solution)/shard_map/reduce_scatter | solution.py:46
  10.8 1.3 copy-start.4
  12.1 158.8 %reduce-scatter.9.cloned.1.call-start = ((), (), s32[]{:S(2)}) async-start(), calls=%async_computation.6 | async-start | bytes 2228224 | tf_op jit(solution)/shard_map/reduce_scatter | solution.py:52
  12.2 3.1 copy-start.3
  12.2 3.1 copy-start.6
  15.3 64.7 %copy-start.1 = (bf16[384,1024]{1,0:T(8,128)(2,1)S(1)}, bf16[384,1024]{1,0:T(8,128)(2,1)}, u32[]{:S(2)}) copy-start(bf16[384,1024]{1,0:T(8,128)(2,1)} %broadcast_select_fusion) | copy-start | bytes 2359300
  84.2 93.1 %copy-start.5 = (s32[512]{0:T(512)S(1)}, s32[512]{0:T(512)}, u32[]{:S(2)}) copy-start(s32[512]{0:T(512)} %param.18) | copy-start | bytes 6148
  84.2 101.8 %copy-start.8 = (f32[384]{0:T(512)S(1)}, f32[384]{0:T(512)}, u32[]{:S(2)}) copy-start(f32[384]{0:T(512)} %param.16) | copy-start | bytes 4612
  172.6 11.2 %all-to-all-start = ((f32[16,1,2048]{2,1,0:T(1,128)}), f32[16,1,2048]{2,1,0:T(1,128)S(1)}, u32[]{:S(2)}, u32[]{:S(2)}) async-start(f32[16,1,2048]{2,1,0:T(1,128)} %reshape.80), calls=%async_computation.2 | async-start | bytes 262144 | tf_op jit(solution)/shard_map/all_to_all | solution.py:55
  177.1 189.7 %reduce-scatter.13.cloned.1.call-start = ((), (), s32[]{:S(2)}) async-start(), calls=%async_computation.8 | async-start | bytes 278528
  305.3 128.5 %copy-start.2 = (bf16[384,1024]{1,0:T(8,128)(2,1)S(1)}, bf16[384,1024]{1,0:T(8,128)(2,1)}, u32[]{:S(2)}) copy-start(bf16[384,1024]{1,0:T(8,128)(2,1)} %broadcast_select_fusion) | copy-start | bytes 2359300
  306.3 199.9 %reduce-scatter.11.cloned.1.call-start = ((), (), s32[]{:S(2)}) async-start(), calls=%async_computation.7 | async-start | bytes 4456448 | tf_op jit(solution)/shard_map/reduce_scatter | solution.py:88
  437.8 68.3 %copy-start.7 = (f32[1024]{0:T(1024)S(1)}, f32[1024]{0:T(1024)}, u32[]{:S(2)}) copy-start(f32[1024]{0:T(1024)} %param.19) | copy-start | bytes 12292
Sparse Core Ops, SparseCore 0:
  12.2 67.7 reduce-scatter.6
  84.3 86.5 reduce-scatter.8
  306.4 60.3 reduce-scatter.12
  438.0 68.1 reduce-scatter.10
